TPU v7x, 256 devices: a whole 4x4x8 slice. The times are simulated.
256 devices in a mesh: ctx: 32 (over z, x), dp: 8 (over y, core).
Axes of the slice: x: 4, y: 4, z: 8, core: 2. Of those that a mesh axis runs over, the one named last changes fastest.
Arguments:
- layer_input: bfloat16 [8, 4096, 5376], P('dp', 'ctx'), may hold values from -12 to 12
- query_states: bfloat16 [8, 4096, 2048], P('dp', 'ctx'), may hold values from -6 to 6
- key_states: bfloat16 [8, 4096, 1024], P('dp', 'ctx'), may hold values from -6 to 6
- value_state_rows: bfloat16 [8, 4096, 1024], P('dp', 'ctx'), may hold values from -6 to 6
- grad_out: bfloat16 [8, 4096, 2048], P('dp', 'ctx'), may hold values from -180 to 180
- segments: int32 [8, 4096], P('dp', 'ctx'), may hold values from 0 to 7, never falling along the last dimension, each value on 1 to 2048 neighbouring positions
- master: float32 [5376, 1024], P(('ctx', 'dp')), may hold values from -0.078125 to 0.078125
- first_moment_value: float32 [5376, 1024], P(('ctx', 'dp')), may hold values from -0.0024 to 0.0024
- second_moment_value: float32 [5376, 1024], P(('ctx', 'dp')), may hold values from 1e-08 to 1e-06
Outputs:
- query_gradient: bfloat16 [8, 4096, 2048], P('dp', 'ctx')
- key_gradient: bfloat16 [8, 4096, 1024], P('dp', 'ctx')
- value_gradient: bfloat16 [8, 4096, 1024], P('dp', 'ctx')
- new_master: float32 [5376, 1024], P(('ctx', 'dp'))
- new_first: float32 [5376, 1024], P(('ctx', 'dp'))
- new_second: float32 [5376, 1024], P(('ctx', 'dp'))
- new_weight: bfloat16 [5376, 1024], P('ctx')
Inputs may be any that keep to these rules, and one draw needn't show every extreme that they name: `segments`: segment numbers never fall along a sequence; each document holds 1 to 2048 tokens and one holds exactly 2048.
All inputs are finite; a program needn't handle non-finite values.
Results may differ from a plain program's by a relative error of at most 0.01.
The roundings to bfloat16 on the way count: a program that leaves them out, or rounds other values in their place, can miss the bound.
Values may be sent and summed in bfloat16 or wider, within the bound.
No kernel may reach another device: no remote copies, remote signals or barrier semaphores. Data moves between devices by JAX's collectives and lax.ppermute only.
A program may use at most 128 MiB of HBM per device.

v0:
```python
import jax
import jax.numpy as jnp
from jax import lax
from jax.sharding import PartitionSpec as P

QUERY_HEADS = 16
KEY_VALUE_HEADS = 8
HEAD_SIZE = 128
WINDOW = 1024
query_scale = 168.0 ** (-0.5)
masked_score = -1e30
clip_norm = 1.0
beta_first = 0.9
beta_second = 0.95
learn_rate = 0.001
decay_rate = 0.1
adam_eps = 1e-08
correct_first = 0.9999734386011124
correct_second = 0.994079470779666


def from_behind(x, axis, by):
    count = lax.axis_size(axis)
    pairs = [(i, i + by) for i in range(count) if 0 <= i + by < count]
    return lax.ppermute(x, axis, pairs)


def attend(
    query_row_block,
    key_row_block,
    value_row_block,
    gradient_rows,
    seg_query,
    seg_key,
    index_query,
    index_key,
):
    shard_length = query_row_block.shape[0]
    extent_rows = key_row_block.shape[0]
    heads_ratio = QUERY_HEADS // KEY_VALUE_HEADS
    query_four_axes = query_row_block.reshape(shard_length, KEY_VALUE_HEADS, heads_ratio, HEAD_SIZE)
    gradient_four_axes = gradient_rows.reshape(
        shard_length, KEY_VALUE_HEADS, heads_ratio, HEAD_SIZE
    )
    key_three_axes = key_row_block.reshape(extent_rows, KEY_VALUE_HEADS, HEAD_SIZE)
    value_three_axes = value_row_block.reshape(extent_rows, KEY_VALUE_HEADS, HEAD_SIZE)
    scores = (
        jnp.einsum(
            "tgrd,egd->grte", query_four_axes, key_three_axes, preferred_element_type=jnp.float32
        )
        * query_scale
    )
    offset = index_query[:, None] - index_key[None, :]
    allowed = (
        (seg_query[:, None] == seg_key[None, :])
        & (offset >= 0)
        & (offset < WINDOW)
        & (index_key[None, :] >= 0)
    )
    scores = jnp.where(allowed, scores, masked_score)
    row_max = jnp.max(scores, axis=-1, keepdims=True)
    weights = jnp.exp(scores - row_max)
    probabilities = weights / jnp.sum(weights, axis=-1, keepdims=True)
    probs_low = probabilities.astype(jnp.bfloat16)
    attn_out = jnp.einsum(
        "grte,egd->tgrd", probs_low, value_three_axes, preferred_element_type=jnp.float32
    )
    row_delta = jnp.sum(gradient_four_axes.astype(jnp.float32) * attn_out, axis=-1)
    grad_probs = jnp.einsum(
        "tgrd,egd->grte", gradient_four_axes, value_three_axes, preferred_element_type=jnp.float32
    )
    grad_scores = probabilities * (grad_probs - jnp.transpose(row_delta, (1, 2, 0))[..., None])
    scores_low = grad_scores.astype(jnp.bfloat16)
    query_gradient = (
        jnp.einsum("grte,egd->tgrd", scores_low, key_three_axes, preferred_element_type=jnp.float32)
        * query_scale
    )
    query_gradient = query_gradient.astype(jnp.bfloat16).reshape(
        shard_length, QUERY_HEADS * HEAD_SIZE
    )
    key_gradient = (
        jnp.einsum(
            "grte,tgrd->egd", scores_low, query_four_axes, preferred_element_type=jnp.float32
        )
        * query_scale
    )
    value_gradient = jnp.einsum(
        "grte,tgrd->egd", probs_low, gradient_four_axes, preferred_element_type=jnp.float32
    )
    return (
        query_gradient,
        key_gradient.reshape(extent_rows, KEY_VALUE_HEADS * HEAD_SIZE),
        value_gradient.reshape(extent_rows, KEY_VALUE_HEADS * HEAD_SIZE),
    )


def shards(
    layer_input,
    query_states,
    key_states,
    value_state_rows,
    grad_out,
    segments,
    master,
    first_moment_value,
    second_moment_value,
):
    shard_length = query_states.shape[1]
    peer_count = min(WINDOW // shard_length, lax.axis_size("ctx") - 1)
    front_len = peer_count * shard_length
    position = lax.axis_index("ctx") * shard_length
    seg_low = segments[0].astype(jnp.bfloat16)
    own_piece = (key_states[0], value_state_rows[0], seg_low)
    incoming_list = []
    for distance in range(peer_count, 0, -1):
        incoming_list.append(
            from_behind((own_piece[0], own_piece[1], own_piece[2]), "ctx", distance)
        )
    halo_rows = tuple(
        (
            jnp.concatenate([incoming[member] for incoming in incoming_list], axis=0)
            for member in range(3)
        )
    )
    key_row_block = jnp.concatenate([halo_rows[0], key_states[0]], axis=0)
    value_row_block = jnp.concatenate([halo_rows[1], value_state_rows[0]], axis=0)
    seg_key = jnp.concatenate([halo_rows[2], seg_low], axis=0)
    index_query = position + jnp.arange(shard_length, dtype=jnp.int32)
    index_key = position - front_len + jnp.arange(front_len + shard_length, dtype=jnp.int32)
    query_gradient, key_gradient, value_gradient = attend(
        query_states[0],
        key_row_block,
        value_row_block,
        grad_out[0],
        seg_low,
        seg_key,
        index_query,
        index_key,
    )
    key_sum = key_gradient[front_len:]
    value_sum = value_gradient[front_len:]
    for distance in range(1, peer_count + 1):
        lower = (peer_count - distance) * shard_length
        key_part = key_gradient[lower : lower + shard_length].astype(jnp.bfloat16)
        value_part = value_gradient[lower : lower + shard_length].astype(jnp.bfloat16)
        returned = from_behind((key_part, value_part), "ctx", -distance)
        key_sum = key_sum + returned[0].astype(jnp.float32)
        value_sum = value_sum + returned[1].astype(jnp.float32)
    key_out = key_sum.astype(jnp.bfloat16)
    value_out = value_sum.astype(jnp.bfloat16)
    feature_block = lax.all_to_all(layer_input[0], "ctx", split_axis=1, concat_axis=0, tiled=True)
    sequence_grad = lax.dot_general(
        feature_block,
        lax.all_gather(value_out, "ctx", axis=0, tiled=True),
        (((0,), (0,)), ((), ())),
        preferred_element_type=jnp.float32,
    )
    weight_grad = lax.psum_scatter(sequence_grad, "dp", scatter_dimension=0, tiled=True)
    square_total = lax.psum(jnp.sum(weight_grad * weight_grad), ("ctx", "dp"))
    norm_total = jnp.sqrt(square_total + 1e-06)
    clipped = weight_grad * jnp.minimum(1.0, clip_norm / norm_total)
    new_first = beta_first * first_moment_value + (1.0 - beta_first) * clipped
    new_second = beta_second * second_moment_value + (1.0 - beta_second) * clipped * clipped
    step_dir = new_first / correct_first / (jnp.sqrt(new_second / correct_second) + adam_eps)
    new_master = master - learn_rate * (step_dir + decay_rate * master)
    new_weight = lax.all_gather(new_master.astype(jnp.bfloat16), "dp", axis=0, tiled=True)
    return (
        query_gradient[None],
        key_out[None],
        value_out[None],
        new_master,
        new_first,
        new_second,
        new_weight,
    )


def solution(mesh):
    return jax.shard_map(
        shards,
        mesh=mesh,
        in_specs=(
            P("dp", "ctx", None),
            P("dp", "ctx", None),
            P("dp", "ctx", None),
            P("dp", "ctx", None),
            P("dp", "ctx", None),
            P("dp", "ctx"),
            P(("ctx", "dp"), None),
            P(("ctx", "dp"), None),
            P(("ctx", "dp"), None),
        ),
        out_specs=(
            P("dp", "ctx", None),
            P("dp", "ctx", None),
            P("dp", "ctx", None),
            P(("ctx", "dp"), None),
            P(("ctx", "dp"), None),
            P(("ctx", "dp"), None),
            P("ctx", None),
        ),
        check_vma=False,
    )
```

profile of v0, /device:TPU:1, one launch (start us, length us, event | category | flops | bytes accessed | tf_op | source)
XLA Modules:
  0.0 551.0 jit_solution(3754582582561746699)
XLA Ops:
  7.9 5.7 %collective-permute-start.8 = (bf16[128]{0:T(256)(128)(2,1)S(1)}, bf16[128]{0:T(256)(128)(2,1)S(1)}, u32[]{:S(2)}, u32[]{:S(2)}) collective-permute-start(bf16[128]{0:T(256)(128)(2,1)S(1)} %convert_bitcast_fusion.1), channel_id=1, source_target_pairs={{0,64},{8,72},{16,80},{24,88},{32,96},{40,104},{48,112},{56,120},{... | collective-permute-start | bytes 776 | tf_op jit(solution)/shard_map/ppermute | solution.py:25
  13.6 5.7 %collective-permute-start.9 = (bf16[128]{0:T(256)(128)(2,1)S(1)}, bf16[128]{0:T(256)(128)(2,1)S(1)}, u32[]{:S(2)}, u32[]{:S(2)}) collective-permute-start(bf16[128]{0:T(256)(128)(2,1)S(1)} %convert_bitcast_fusion.1), channel_id=1, source_target_pairs={{0,56},{8,64},{16,72},{24,80},{32,88},{40,96},{48,104},{56,112},{6... | collective-permute-start | bytes 776 | tf_op jit(solution)/shard_map/ppermute | solution.py:25
  21.1 5.2 collective-permute-start
  26.4 3.4 collective-permute-start.1
  36.5 3.6 collective-permute-start.10
  42.9 8.8 %collective-permute-start.12 = (bf16[128]{0:T(256)(128)(2,1)S(1)}, bf16[128]{0:T(256)(128)(2,1)S(1)}, u32[]{:S(2)}, u32[]{:S(2)}) collective-permute-start(bf16[128]{0:T(256)(128)(2,1)S(1)} %convert_bitcast_fusion.1), channel_id=1, source_target_pairs={{0,32},{8,40},{16,48},{24,56},{32,64},{40,72},{48,80},{56,88},{64,... | collective-permute-start | bytes 776 | tf_op jit(solution)/shard_map/ppermute | solution.py:25
  52.0 14.1 %collective-permute-start.13 = (bf16[128]{0:T(256)(128)(2,1)S(1)}, bf16[128]{0:T(256)(128)(2,1)S(1)}, u32[]{:S(2)}, u32[]{:S(2)}) collective-permute-start(bf16[128]{0:T(256)(128)(2,1)S(1)} %convert_bitcast_fusion.1), channel_id=1, source_target_pairs={{0,24},{8,32},{16,40},{24,48},{32,56},{40,64},{48,72},{56,80},{64,... | collective-permute-start | bytes 776 | tf_op jit(solution)/shard_map/ppermute | solution.py:25
  67.9 3.1 collective-permute-start.15
  71.3 7.6 %collective-permute-start.3 = (bf16[128,1024]{0,1:T(8,128)(2,1)}, bf16[128,1024]{0,1:T(8,128)(2,1)S(1)}, u32[]{:S(2)}, u32[]{:S(2)}) collective-permute-start(bf16[128,1024]{0,1:T(8,128)(2,1)} %bitcast), channel_id=1, source_target_pairs={{0,40},{8,48},{16,56},{24,64},{32,72},{40,80},{48,88},{56,96},{64,... | collective-permute-start | bytes 786440 | tf_op jit(solution)/shard_map/ppermute | solution.py:25
  82.2 3.5 collective-permute-start.5
  88.8 3.2 collective-permute-start.7
  107.0 6.1 %fusion.54 = (f32[8,2,128]{2,1,0:T(2,128)}, f32[8,2,128,1152]{2,3,1,0:T(8,128)}) fusion(pred[128,1152]{0,1:T(8,128)(4,1)S(1)} %fusion.40, bf16[128,8,2,128]{0,3,2,1:T(8,128)(2,1)S(1)} %bitcast.154, bf16[1152,8,128]{2,0,1:T(8,128)(2,1)S(1)} %constant_dynamic-update-slice_fusion), kind=kOutput, calls=%fused_computation.72 | convolution fusion | flops 613418112 | bytes 12476416 | tf_op jit(solution)/shard_map/sub | solution.py:62
  113.1 4.8 fusion.9
  117.9 3.7 fusion.58
  140.2 28.3 %collective-permute-done.39 = bf16[128,1024]{1,0:T(8,128)(2,1)} collective-permute-done((bf16[128,1024]{1,0:T(8,128)(2,1)}, bf16[128,1024]{1,0:T(8,128)(2,1)}, u32[]{:S(2)}, u32[]{:S(2)}) %collective-permute-start.39) | collective-permute-done | bytes 262176 | tf_op jit(solution)/shard_map/ppermute | solution.py:25
  173.9 10.8 %collective-permute-done.34 = bf16[128,1024]{1,0:T(8,128)(2,1)} collective-permute-done((bf16[128,1024]{1,0:T(8,128)(2,1)}, bf16[128,1024]{1,0:T(8,128)(2,1)}, u32[]{:S(2)}, u32[]{:S(2)}) %collective-permute-start.34) | collective-permute-done | bytes 262176 | tf_op jit(solution)/shard_map/ppermute | solution.py:25
  184.7 4.5 collective-permute-done.32
  192.6 25.7 %collective-permute-start.16 = (bf16[128,1024]{0,1:T(8,128)(2,1)}, bf16[128,1024]{0,1:T(8,128)(2,1)}, u32[]{:S(2)}, u32[]{:S(2)}) collective-permute-start(bf16[128,1024]{0,1:T(8,128)(2,1)} %bitcast.15), channel_id=1, source_target_pairs={{0,64},{8,72},{16,80},{24,88},{32,96},{40,104},{48,112},{56,120},{... | collective-permute-start | bytes 786440 | tf_op jit(solution)/shard_map/ppermute | solution.py:25
  218.4 7.7 %collective-permute-start.17 = (bf16[128,1024]{0,1:T(8,128)(2,1)}, bf16[128,1024]{0,1:T(8,128)(2,1)}, u32[]{:S(2)}, u32[]{:S(2)}) collective-permute-start(bf16[128,1024]{0,1:T(8,128)(2,1)} %bitcast.15), channel_id=1, source_target_pairs={{0,56},{8,64},{16,72},{24,80},{32,88},{40,96},{48,104},{56,112},{6... | collective-permute-start | bytes 786440 | tf_op jit(solution)/shard_map/ppermute | solution.py:25
  232.5 3.8 collective-permute-start.21
  238.6 3.2 collective-permute-done.18
  246.4 31.1 %all-to-all-start = ((bf16[128,32,168]{0,2,1:T(8,128)(2,1)}), bf16[128,32,168]{0,2,1:T(8,128)(2,1)}, u32[]{:S(2)}, u32[]{:S(2)}) async-start(bf16[128,32,168]{0,2,1:T(8,128)(2,1)} %bitcast.152), calls=%async_computation | async-start | bytes 2752512 | tf_op jit(solution)/shard_map/all_to_all | solution.py:151
  299.1 3.5 fusion.35
  305.6 3.7 fusion.57
  320.1 42.3 %all-gather.3.cloned.1.call-done = bf16[4096,1024]{1,0:T(8,128)(2,1)} async-done(((bf16[128,1024]{1,0:T(8,128)(2,1)}), bf16[4096,1024]{1,0:T(8,128)(2,1)}) %all-gather.3.cloned.1.call-update) | async-done | bytes 8388624 | tf_op jit(solution)/shard_map/all_gather | solution.py:154
  362.4 6.2 %fusion.32 = f32[168,1024]{1,0:T(8,128)} fusion(bf16[4096,1024]{1,0:T(8,128)(2,1)} %all-gather.3.cloned.1.call-done, bf16[128,32,168]{0,2,1:T(8,128)(2,1)} %all-to-all-done), kind=kOutput, calls=%fused_computation.29 | convolution fusion | flops 1409286144 | bytes 10452992 | tf_op jit(solution)/shard_map/dot_general | solution.py:152
  368.5 18.3 %fusion = f32[24,1024]{1,0:T(8,128)S(1)} fusion(f32[168,1024]{1,0:T(8,128)} %fusion.32), kind=kCustom, calls=%all-reduce-scatter | all-reduce-scatter fusion | flops 196609 | bytes 787456
  402.1 3.4 fusion.29
  409.4 12.0 %collective-permute-done.28 = bf16[128,1024]{1,0:T(8,128)(2,1)} collective-permute-done((bf16[128,1024]{1,0:T(8,128)(2,1)}, bf16[128,1024]{1,0:T(8,128)(2,1)}, u32[]{:S(2)}, u32[]{:S(2)}) %collective-permute-start.28) | collective-permute-done | bytes 262176 | tf_op jit(solution)/shard_map/ppermute | solution.py:25
  421.5 7.7 %collective-permute-done.24 = bf16[128,1024]{1,0:T(8,128)(2,1)} collective-permute-done((bf16[128,1024]{1,0:T(8,128)(2,1)S(1)}, bf16[128,1024]{1,0:T(8,128)(2,1)}, u32[]{:S(2)}, u32[]{:S(2)}) %collective-permute-start.24) | collective-permute-done | bytes 262176 | tf_op jit(solution)/shard_map/ppermute | solution.py:25
  431.7 96.6 %psum.7 = f32[]{:T(128)} all-reduce(f32[]{:T(128)} %multiply_reduce_fusion), channel_id=1, replica_groups=mesh['ctx'=32,'dp'=8] {'ctx','dp'}, use_global_device_ids=true, to_apply=%region_5.6 | all-reduce | flops 1 | bytes 8 | tf_op jit(solution)/shard_map/psum | solution.py:159
  529.8 13.5 %all-gather = bf16[8,21,1024]{2,1,0:T(8,128)(2,1)S(1)} all-gather(bf16[1,21,1024]{2,1,0:T(8,128)(2,1)S(1)} %get-tuple-element.28), channel_id=1, replica_groups=mesh['ctx'=32,'dp'=8] {'dp'}, dimensions={0}, use_global_device_ids=true | all-gather | bytes 387072 | tf_op jit(solution)/shard_map/all_gather | solution.py:166
  (200 shorter events, 133.8 us)
Async XLA Ops:
  7.2 355.2 %all-gather.3.cloned.1.call-start = ((), (), s32[]{:S(2)}) async-start(), calls=%async_computation.1 | async-start | bytes 8650752 | tf_op jit(solution)/shard_map/all_gather | solution.py:154
  7.9 28.6 %collective-permute-start.8 = (bf16[128]{0:T(256)(128)(2,1)S(1)}, bf16[128]{0:T(256)(128)(2,1)S(1)}, u32[]{:S(2)}, u32[]{:S(2)}) collective-permute-start(bf16[128]{0:T(256)(128)(2,1)S(1)} %convert_bitcast_fusion.1), channel_id=1, source_target_pairs={{0,64},{8,72},{16,80},{24,88},{32,96},{40,104},{48,112},{56,120},{... | collective-permute-start | bytes 776 | tf_op jit(solution)/shard_map/ppermute | solution.py:25
  13.6 26.8 %collective-permute-start.9 = (bf16[128]{0:T(256)(128)(2,1)S(1)}, bf16[128]{0:T(256)(128)(2,1)S(1)}, u32[]{:S(2)}, u32[]{:S(2)}) collective-permute-start(bf16[128]{0:T(256)(128)(2,1)S(1)} %convert_bitcast_fusion.1), channel_id=1, source_target_pairs={{0,56},{8,64},{16,72},{24,80},{32,88},{40,96},{48,104},{56,112},{6... | collective-permute-start | bytes 776 | tf_op jit(solution)/shard_map/ppermute | solution.py:25
  21.1 61.1 %collective-permute-start = (bf16[128,1024]{0,1:T(8,128)(2,1)}, bf16[128,1024]{0,1:T(8,128)(2,1)S(1)}, u32[]{:S(2)}, u32[]{:S(2)}) collective-permute-start(bf16[128,1024]{0,1:T(8,128)(2,1)} %bitcast), channel_id=1, source_target_pairs={{0,64},{8,72},{16,80},{24,88},{32,96},{40,104},{48,112},{56,120},{... | collective-permute-start | bytes 786440 | tf_op jit(solution)/shard_map/ppermute | solution.py:25
  26.4 59.3 %collective-permute-start.1 = (bf16[128,1024]{0,1:T(8,128)(2,1)}, bf16[128,1024]{0,1:T(8,128)(2,1)S(1)}, u32[]{:S(2)}, u32[]{:S(2)}) collective-permute-start(bf16[128,1024]{0,1:T(8,128)(2,1)} %bitcast), channel_id=1, source_target_pairs={{0,56},{8,64},{16,72},{24,80},{32,88},{40,96},{48,104},{56,112},{6... | collective-permute-start | bytes 786440 | tf_op jit(solution)/shard_map/ppermute | solution.py:25
  29.8 59.0 %collective-permute-start.2 = (bf16[128,1024]{0,1:T(8,128)(2,1)}, bf16[128,1024]{0,1:T(8,128)(2,1)S(1)}, u32[]{:S(2)}, u32[]{:S(2)}) collective-permute-start(bf16[128,1024]{0,1:T(8,128)(2,1)} %bitcast), channel_id=1, source_target_pairs={{0,48},{8,56},{16,64},{24,72},{32,80},{40,88},{48,96},{56,104},{64... | collective-permute-start | bytes 786440 | tf_op jit(solution)/shard_map/ppermute | solution.py:25
  42.9 23.5 %collective-permute-start.12 = (bf16[128]{0:T(256)(128)(2,1)S(1)}, bf16[128]{0:T(256)(128)(2,1)S(1)}, u32[]{:S(2)}, u32[]{:S(2)}) collective-permute-start(bf16[128]{0:T(256)(128)(2,1)S(1)} %convert_bitcast_fusion.1), channel_id=1, source_target_pairs={{0,32},{8,40},{16,48},{24,56},{32,64},{40,72},{48,80},{56,88},{64,... | collective-permute-start | bytes 776 | tf_op jit(solution)/shard_map/ppermute | solution.py:25
  71.3 24.3 %collective-permute-start.3 = (bf16[128,1024]{0,1:T(8,128)(2,1)}, bf16[128,1024]{0,1:T(8,128)(2,1)S(1)}, u32[]{:S(2)}, u32[]{:S(2)}) collective-permute-start(bf16[128,1024]{0,1:T(8,128)(2,1)} %bitcast), channel_id=1, source_target_pairs={{0,40},{8,48},{16,56},{24,64},{32,72},{40,80},{48,88},{56,96},{64,... | collective-permute-start | bytes 786440 | tf_op jit(solution)/shard_map/ppermute | solution.py:25
  79.1 17.3 %collective-permute-start.4 = (bf16[128,1024]{0,1:T(8,128)(2,1)}, bf16[128,1024]{0,1:T(8,128)(2,1)S(1)}, u32[]{:S(2)}, u32[]{:S(2)}) collective-permute-start(bf16[128,1024]{0,1:T(8,128)(2,1)} %bitcast), channel_id=1, source_target_pairs={{0,32},{8,40},{16,48},{24,56},{32,64},{40,72},{48,80},{56,88},{64,... | collective-permute-start | bytes 786440 | tf_op jit(solution)/shard_map/ppermute | solution.py:25
  124.9 43.6 %collective-permute-start.39 = (bf16[128,1024]{1,0:T(8,128)(2,1)}, bf16[128,1024]{1,0:T(8,128)(2,1)}, u32[]{:S(2)}, u32[]{:S(2)}) collective-permute-start(bf16[128,1024]{1,0:T(8,128)(2,1)} %copy.147), channel_id=1, source_target_pairs={{64,0},{72,8},{80,16},{88,24},{96,32},{104,40},{112,48},{120,56},{... | collective-permute-start | bytes 786440 | tf_op jit(solution)/shard_map/ppermute | solution.py:25
  128.0 41.8 %collective-permute-start.38 = (bf16[128,1024]{1,0:T(8,128)(2,1)}, bf16[128,1024]{1,0:T(8,128)(2,1)}, u32[]{:S(2)}, u32[]{:S(2)}) collective-permute-start(bf16[128,1024]{1,0:T(8,128)(2,1)} %copy.146), channel_id=1, source_target_pairs={{56,0},{64,8},{72,16},{80,24},{88,32},{96,40},{104,48},{112,56},{1... | collective-permute-start | bytes 786440 | tf_op jit(solution)/shard_map/ppermute | solution.py:25
  131.1 40.0 %collective-permute-start.37 = (bf16[128,1024]{1,0:T(8,128)(2,1)}, bf16[128,1024]{1,0:T(8,128)(2,1)}, u32[]{:S(2)}, u32[]{:S(2)}) collective-permute-start(bf16[128,1024]{1,0:T(8,128)(2,1)} %copy.145), channel_id=1, source_target_pairs={{48,0},{56,8},{64,16},{72,24},{80,32},{88,40},{96,48},{104,56},{11... | collective-permute-start | bytes 786440 | tf_op jit(solution)/shard_map/ppermute | solution.py:25
  134.1 39.7 %collective-permute-start.36 = (bf16[128,1024]{1,0:T(8,128)(2,1)}, bf16[128,1024]{1,0:T(8,128)(2,1)}, u32[]{:S(2)}, u32[]{:S(2)}) collective-permute-start(bf16[128,1024]{1,0:T(8,128)(2,1)} %copy.144), channel_id=1, source_target_pairs={{40,0},{48,8},{56,16},{64,24},{72,32},{80,40},{88,48},{96,56},{104... | collective-permute-start | bytes 786440 | tf_op jit(solution)/shard_map/ppermute | solution.py:25
  136.3 37.6 %collective-permute-start.35 = (bf16[128,1024]{1,0:T(8,128)(2,1)}, bf16[128,1024]{1,0:T(8,128)(2,1)}, u32[]{:S(2)}, u32[]{:S(2)}) collective-permute-start(bf16[128,1024]{1,0:T(8,128)(2,1)} %copy.143), channel_id=1, source_target_pairs={{32,0},{40,8},{48,16},{56,24},{64,32},{72,40},{80,48},{88,56},{96,... | collective-permute-start | bytes 786440 | tf_op jit(solution)/shard_map/ppermute | solution.py:25
  168.5 16.2 %collective-permute-start.34 = (bf16[128,1024]{1,0:T(8,128)(2,1)}, bf16[128,1024]{1,0:T(8,128)(2,1)}, u32[]{:S(2)}, u32[]{:S(2)}) collective-permute-start(bf16[128,1024]{1,0:T(8,128)(2,1)} %copy.142), channel_id=1, source_target_pairs={{24,0},{32,8},{40,16},{48,24},{56,32},{64,40},{72,48},{80,56},{88,... | collective-permute-start | bytes 786440 | tf_op jit(solution)/shard_map/ppermute | solution.py:25
  171.1 18.1 %collective-permute-start.32 = (bf16[128,1024]{1,0:T(8,128)(2,1)}, bf16[128,1024]{1,0:T(8,128)(2,1)}, u32[]{:S(2)}, u32[]{:S(2)}) collective-permute-start(bf16[128,1024]{1,0:T(8,128)(2,1)} %copy.139), channel_id=1, source_target_pairs={{8,0},{16,8},{24,16},{32,24},{40,32},{48,40},{56,48},{64,56},{72,6... | collective-permute-start | bytes 786440 | tf_op jit(solution)/shard_map/ppermute | solution.py:25
  192.6 39.8 %collective-permute-start.16 = (bf16[128,1024]{0,1:T(8,128)(2,1)}, bf16[128,1024]{0,1:T(8,128)(2,1)}, u32[]{:S(2)}, u32[]{:S(2)}) collective-permute-start(bf16[128,1024]{0,1:T(8,128)(2,1)} %bitcast.15), channel_id=1, source_target_pairs={{0,64},{8,72},{16,80},{24,88},{32,96},{40,104},{48,112},{56,120},{... | collective-permute-start | bytes 786440 | tf_op jit(solution)/shard_map/ppermute | solution.py:25
  218.4 17.9 %collective-permute-start.17 = (bf16[128,1024]{0,1:T(8,128)(2,1)}, bf16[128,1024]{0,1:T(8,128)(2,1)}, u32[]{:S(2)}, u32[]{:S(2)}) collective-permute-start(bf16[128,1024]{0,1:T(8,128)(2,1)} %bitcast.15), channel_id=1, source_target_pairs={{0,56},{8,64},{16,72},{24,80},{32,88},{40,96},{48,104},{56,112},{6... | collective-permute-start | bytes 786440 | tf_op jit(solution)/shard_map/ppermute | solution.py:25
  228.1 56.7 %collective-permute-start.19 = (bf16[128,1024]{0,1:T(8,128)(2,1)}, bf16[128,1024]{0,1:T(8,128)(2,1)}, u32[]{:S(2)}, u32[]{:S(2)}) collective-permute-start(bf16[128,1024]{0,1:T(8,128)(2,1)} %bitcast.15), channel_id=1, source_target_pairs={{0,40},{8,48},{16,56},{24,64},{32,72},{40,80},{48,88},{56,96},{64,... | collective-permute-start | bytes 786440 | tf_op jit(solution)/shard_map/ppermute | solution.py:25
  230.1 56.5 %collective-permute-start.20 = (bf16[128,1024]{0,1:T(8,128)(2,1)}, bf16[128,1024]{0,1:T(8,128)(2,1)}, u32[]{:S(2)}, u32[]{:S(2)}) collective-permute-start(bf16[128,1024]{0,1:T(8,128)(2,1)} %bitcast.15), channel_id=1, source_target_pairs={{0,32},{8,40},{16,48},{24,56},{32,64},{40,72},{48,80},{56,88},{64,... | collective-permute-start | bytes 786440 | tf_op jit(solution)/shard_map/ppermute | solution.py:25
  232.5 55.9 %collective-permute-start.21 = (bf16[128,1024]{0,1:T(8,128)(2,1)}, bf16[128,1024]{0,1:T(8,128)(2,1)}, u32[]{:S(2)}, u32[]{:S(2)}) collective-permute-start(bf16[128,1024]{0,1:T(8,128)(2,1)} %bitcast.15), channel_id=1, source_target_pairs={{0,24},{8,32},{16,40},{24,48},{32,56},{40,64},{48,72},{56,80},{64,... | collective-permute-start | bytes 786440 | tf_op jit(solution)/shard_map/ppermute | solution.py:25
  236.3 54.0 %collective-permute-start.22 = (bf16[128,1024]{0,1:T(8,128)(2,1)}, bf16[128,1024]{0,1:T(8,128)(2,1)}, u32[]{:S(2)}, u32[]{:S(2)}) collective-permute-start(bf16[128,1024]{0,1:T(8,128)(2,1)} %bitcast.15), channel_id=1, source_target_pairs={{0,16},{8,24},{16,32},{24,40},{32,48},{40,56},{48,64},{56,72},{64,... | collective-permute-start | bytes 786440 | tf_op jit(solution)/shard_map/ppermute | solution.py:25
  241.9 50.1 %collective-permute-start.23 = (bf16[128,1024]{0,1:T(8,128)(2,1)}, bf16[128,1024]{0,1:T(8,128)(2,1)}, u32[]{:S(2)}, u32[]{:S(2)}) collective-permute-start(bf16[128,1024]{0,1:T(8,128)(2,1)} %bitcast.15), channel_id=1, source_target_pairs={{0,8},{8,16},{16,24},{24,32},{32,40},{40,48},{48,56},{56,64},{64,7... | collective-permute-start | bytes 786440 | tf_op jit(solution)/shard_map/ppermute | solution.py:25
  246.4 73.7 %all-to-all-start = ((bf16[128,32,168]{0,2,1:T(8,128)(2,1)}), bf16[128,32,168]{0,2,1:T(8,128)(2,1)}, u32[]{:S(2)}, u32[]{:S(2)}) async-start(bf16[128,32,168]{0,2,1:T(8,128)(2,1)} %bitcast.152), calls=%async_computation | async-start | bytes 2752512 | tf_op jit(solution)/shard_map/all_to_all | solution.py:151
  312.5 84.1 %collective-permute-start.31 = (bf16[128,1024]{1,0:T(8,128)(2,1)}, bf16[128,1024]{1,0:T(8,128)(2,1)}, u32[]{:S(2)}, u32[]{:S(2)}) collective-permute-start(bf16[128,1024]{1,0:T(8,128)(2,1)} %copy.137), channel_id=1, source_target_pairs={{64,0},{72,8},{80,16},{88,24},{96,32},{104,40},{112,48},{120,56},{... | collective-permute-start | bytes 786440 | tf_op jit(solution)/shard_map/ppermute | solution.py:25
  315.6 82.3 %collective-permute-start.30 = (bf16[128,1024]{1,0:T(8,128)(2,1)}, bf16[128,1024]{1,0:T(8,128)(2,1)}, u32[]{:S(2)}, u32[]{:S(2)}) collective-permute-start(bf16[128,1024]{1,0:T(8,128)(2,1)} %copy.136), channel_id=1, source_target_pairs={{56,0},{64,8},{72,16},{80,24},{88,32},{96,40},{104,48},{112,56},{1... | collective-permute-start | bytes 786440 | tf_op jit(solution)/shard_map/ppermute | solution.py:25
  318.7 80.5 %collective-permute-start.29 = (bf16[128,1024]{1,0:T(8,128)(2,1)}, bf16[128,1024]{1,0:T(8,128)(2,1)}, u32[]{:S(2)}, u32[]{:S(2)}) collective-permute-start(bf16[128,1024]{1,0:T(8,128)(2,1)} %copy.135), channel_id=1, source_target_pairs={{48,0},{56,8},{64,16},{72,24},{80,32},{88,40},{96,48},{104,56},{11... | collective-permute-start | bytes 786440 | tf_op jit(solution)/shard_map/ppermute | solution.py:25
  393.3 28.1 %collective-permute-start.28 = (bf16[128,1024]{1,0:T(8,128)(2,1)}, bf16[128,1024]{1,0:T(8,128)(2,1)}, u32[]{:S(2)}, u32[]{:S(2)}) collective-permute-start(bf16[128,1024]{1,0:T(8,128)(2,1)} %copy.134), channel_id=1, source_target_pairs={{40,0},{48,8},{56,16},{64,24},{72,32},{80,40},{88,48},{96,56},{104... | collective-permute-start | bytes 786440 | tf_op jit(solution)/shard_map/ppermute | solution.py:25
  396.6 24.8 %collective-permute-start.27 = (bf16[128,1024]{1,0:T(8,128)(2,1)}, bf16[128,1024]{1,0:T(8,128)(2,1)}, u32[]{:S(2)}, u32[]{:S(2)}) collective-permute-start(bf16[128,1024]{1,0:T(8,128)(2,1)} %copy.133), channel_id=1, source_target_pairs={{32,0},{40,8},{48,16},{56,24},{64,32},{72,40},{80,48},{88,56},{96,... | collective-permute-start | bytes 786440 | tf_op jit(solution)/shard_map/ppermute | solution.py:25
  397.9 23.5 %collective-permute-start.26 = (bf16[128,1024]{1,0:T(8,128)(2,1)}, bf16[128,1024]{1,0:T(8,128)(2,1)}, u32[]{:S(2)}, u32[]{:S(2)}) collective-permute-start(bf16[128,1024]{1,0:T(8,128)(2,1)} %copy.132), channel_id=1, source_target_pairs={{24,0},{32,8},{40,16},{48,24},{56,32},{64,40},{72,48},{80,56},{88,... | collective-permute-start | bytes 786440 | tf_op jit(solution)/shard_map/ppermute | solution.py:25
  399.2 22.2 %collective-permute-start.25 = (bf16[128,1024]{1,0:T(8,128)(2,1)S(1)}, bf16[128,1024]{1,0:T(8,128)(2,1)}, u32[]{:S(2)}, u32[]{:S(2)}) collective-permute-start(bf16[128,1024]{1,0:T(8,128)(2,1)S(1)} %copy.131), channel_id=1, source_target_pairs={{16,0},{24,8},{32,16},{40,24},{48,32},{56,40},{64,48},{72,56},{80,... | collective-permute-start | bytes 786440 | tf_op jit(solution)/shard_map/ppermute | solution.py:25
  400.5 28.6 %collective-permute-start.24 = (bf16[128,1024]{1,0:T(8,128)(2,1)S(1)}, bf16[128,1024]{1,0:T(8,128)(2,1)}, u32[]{:S(2)}, u32[]{:S(2)}) collective-permute-start(bf16[128,1024]{1,0:T(8,128)(2,1)S(1)} %copy.129), channel_id=1, source_target_pairs={{8,0},{16,8},{24,16},{32,24},{40,32},{48,40},{56,48},{64,56},{72,6... | collective-permute-start | bytes 786440 | tf_op jit(solution)/shard_map/ppermute | solution.py:25
  (34 other events, 907.8 us)
Sparse Core Ops, SparseCore 0:
  191.9 170.4 all-gather.2
where the time goes:
time: 554 us; the launch traced here: 551 us
  starting transfers between devices  178 us (32%)
  blocking collectives  128 us (23%)
  waiting for transfers between devices  109 us (20%)
  local copies, waits for them, and re-layouts  77.8 us (14%)
  matrix products  28.2 us (5%)
  between operations  16.3 us (3%)
  other arithmetic  13.1 us (2%)
    ppermute x40, starting transfers between devices, from_behind(): return lax.ppermute(x, axis, pairs)  144 us
    psum x1, blocking collectives, shards(): square_total = lax.psum(jnp.sum(weight_grad * weight_grad), ('ctx', 'dp'))  96.6 us
    ppermute x40, waiting for transfers between devices, from_behind(): return lax.ppermute(x, axis, pairs)  66.6 us
    all_gather x1, waiting for transfers between devices, shards(): lax.all_gather(value_out, 'ctx', axis=0, tiled=True)  42.3 us
    all_to_all x1, starting transfers between devices, shards(): lax.all_to_all(layer_input[0], 'ctx', split_axis=1, concat_axis=0, tiled=...  31.1 us
    unnamed x79, local copies, waits for them, and re-layouts  25.1 us
    unnamed x1, blocking collectives  18.3 us
    concatenate x10, local copies, waits for them, and re-layouts, shards(): jnp.concatenate([halo_rows[1], value_state_rows[0]], axis=0)  16.3 us
  transfers between devices with their start and end apart: 43, of which 7 were waited for; matrix products, arithmetic and copies ran while one was open for 19% of the time, Pallas kernels for 0%

commit v1 on v0

--- a/solution.py
+++ b/solution.py
@@ -151,7 +151,9 @@
     feature_block = lax.all_to_all(layer_input[0], "ctx", split_axis=1, concat_axis=0, tiled=True)
     sequence_grad = lax.dot_general(
         feature_block,
-        lax.all_gather(value_out, "ctx", axis=0, tiled=True),
+        jnp.concatenate(
+            lax.all_to_all(jnp.stack([value_out] * lax.axis_size("ctx")), "ctx", 0, 0), axis=0
+        ),
         (((0,), (0,)), ((), ())),
         preferred_element_type=jnp.float32,
     )

time: 554 us -> 700 us (1.26)
  waiting for transfers between devices: 109 us -> 253 us
  between operations: 16.3 us -> 2.92 us
  blocking collectives: 128 us -> 135 us
    ppermute x40, waiting for transfers between devices: 66.6 us -> 253 us  [from_behind(): return lax.ppermute(x, axis, pairs)]
    all_gather x1 -> x0, waiting for transfers between devices: 42.3 us -> none  [shards(): lax.all_gather(value_out, 'ctx', axis=0, tiled=True)]
    all_to_all x0 -> x1, starting transfers between devices: none -> 30.3 us  [shards(): lax.all_to_all(jnp.stack([value_out] * lax.axis_size('ctx')), 'ctx', 0, 0)]
    all_to_all x1, starting transfers between devices: 31.1 us -> 4.96 us  [shards(): lax.all_to_all(layer_input[0], 'ctx', split_axis=1, concat_axis=0, tiled=...]
    unnamed x79 -> x91, local copies, waits for them, and re-layouts: 25.1 us -> 24 us
  transfers between devices with their start and end apart: 43 -> 43, of which waited for: 7 -> 9; matrix products, arithmetic and copies ran while one was open for 19% -> 19% of each run, Pallas kernels for 0% -> 0%
where the time goes in v1:
time: 700 us; the launch traced here: 697 us
  waiting for transfers between devices  253 us (36%)
  starting transfers between devices  184 us (26%)
  blocking collectives  135 us (19%)
  local copies, waits for them, and re-layouts  81.2 us (12%)
  matrix products  28.2 us (4%)
  other arithmetic  12.4 us (2%)
    ppermute x40, waiting for transfers between devices, from_behind(): return lax.ppermute(x, axis, pairs)  253 us
    ppermute x40, starting transfers between devices, from_behind(): return lax.ppermute(x, axis, pairs)  147 us
    psum x1, blocking collectives, shards(): square_total = lax.psum(jnp.sum(weight_grad * weight_grad), ('ctx', 'dp'))  103 us
    all_to_all x1, starting transfers between devices, shards(): lax.all_to_all(jnp.stack([value_out] * lax.axis_size('ctx')), 'ctx', 0, 0)  30.3 us
    unnamed x91, local copies, waits for them, and re-layouts  24 us
    unnamed x1, blocking collectives  18.2 us
    concatenate x10, local copies, waits for them, and re-layouts, shards(): jnp.concatenate([halo_rows[1], value_state_rows[0]], axis=0)  16.2 us
  transfers between devices with their start and end apart: 43, of which 9 were waited for; matrix products, arithmetic and copies ran while one was open for 19% of the time, Pallas kernels for 0%

profile of v1, /device:TPU:1, one launch (start us, length us, event | category | flops | bytes accessed | tf_op | source)
XLA Modules:
  0.0 696.8 jit_solution(5819781610760682019)
XLA Ops:
  1.3 5.7 collective-permute-start.8
  7.0 5.7 collective-permute-start.9
  14.5 5.3 collective-permute-start
  27.7 5.0 all-to-all-start.1
  35.3 5.5 collective-permute-start.10
  44.4 21.3 %collective-permute-done.10 = bf16[128]{0:T(256)(128)(2,1)S(1)} collective-permute-done((bf16[128]{0:T(256)(128)(2,1)S(1)}, bf16[128]{0:T(256)(128)(2,1)S(1)}, u32[]{:S(2)}, u32[]{:S(2)}) %collective-permute-start.10) | collective-permute-done | bytes 288 | tf_op jit(solution)/shard_map/ppermute | solution.py:25
  65.6 9.8 %collective-permute-start.12 = (bf16[128]{0:T(256)(128)(2,1)S(1)}, bf16[128]{0:T(256)(128)(2,1)S(1)}, u32[]{:S(2)}, u32[]{:S(2)}) collective-permute-start(bf16[128]{0:T(256)(128)(2,1)S(1)} %convert_bitcast_fusion.1), channel_id=1, source_target_pairs={{0,32},{8,40},{16,48},{24,56},{32,64},{40,72},{48,80},{56,88},{64,... | collective-permute-start | bytes 776 | tf_op jit(solution)/shard_map/ppermute | solution.py:25
  75.7 13.9 %collective-permute-start.13 = (bf16[128]{0:T(256)(128)(2,1)S(1)}, bf16[128]{0:T(256)(128)(2,1)S(1)}, u32[]{:S(2)}, u32[]{:S(2)}) collective-permute-start(bf16[128]{0:T(256)(128)(2,1)S(1)} %convert_bitcast_fusion.1), channel_id=1, source_target_pairs={{0,24},{8,32},{16,40},{24,48},{32,56},{40,64},{48,72},{56,80},{64,... | collective-permute-start | bytes 776 | tf_op jit(solution)/shard_map/ppermute | solution.py:25
  94.7 7.3 %collective-permute-start.3 = (bf16[128,1024]{0,1:T(8,128)(2,1)}, bf16[128,1024]{0,1:T(8,128)(2,1)S(1)}, u32[]{:S(2)}, u32[]{:S(2)}) collective-permute-start(bf16[128,1024]{0,1:T(8,128)(2,1)} %bitcast), channel_id=1, source_target_pairs={{0,40},{8,48},{16,56},{24,64},{32,72},{40,80},{48,88},{56,96},{64,... | collective-permute-start | bytes 786440 | tf_op jit(solution)/shard_map/ppermute | solution.py:25
  129.6 6.1 fusion.53
  135.7 4.8 fusion.9
  140.5 3.7 fusion.57
  162.8 28.2 %collective-permute-done.39 = bf16[128,1024]{1,0:T(8,128)(2,1)} collective-permute-done((bf16[128,1024]{1,0:T(8,128)(2,1)}, bf16[128,1024]{1,0:T(8,128)(2,1)}, u32[]{:S(2)}, u32[]{:S(2)}) %collective-permute-start.39) | collective-permute-done | bytes 262176 | tf_op jit(solution)/shard_map/ppermute | solution.py:25
  196.2 10.7 %collective-permute-done.34 = bf16[128,1024]{1,0:T(8,128)(2,1)} collective-permute-done((bf16[128,1024]{1,0:T(8,128)(2,1)}, bf16[128,1024]{1,0:T(8,128)(2,1)}, u32[]{:S(2)}, u32[]{:S(2)}) %collective-permute-start.34) | collective-permute-done | bytes 262176 | tf_op jit(solution)/shard_map/ppermute | solution.py:25
  206.9 4.7 collective-permute-done.32
  213.6 4.4 stack.2
  218.0 30.3 %all-to-all-start = ((bf16[32,128,1024]{2,1,0:T(8,128)(2,1)}), bf16[32,128,1024]{2,1,0:T(8,128)(2,1)}, u32[]{:S(2)}, u32[]{:S(2)}) async-start(bf16[32,128,1024]{2,1,0:T(8,128)(2,1)} %stack.2), calls=%async_computation | async-start | bytes 16777216 | tf_op jit(solution)/shard_map/all_to_all | solution.py:155
  249.1 4.0 collective-permute-start.16
  253.1 5.2 collective-permute-start.17
  258.3 4.6 collective-permute-start.18
  269.1 168.1 %collective-permute-done.16 = bf16[128,1024]{0,1:T(8,128)(2,1)S(1)} collective-permute-done((bf16[128,1024]{0,1:T(8,128)(2,1)}, bf16[128,1024]{0,1:T(8,128)(2,1)S(1)}, u32[]{:S(2)}, u32[]{:S(2)}) %collective-permute-start.16) | collective-permute-done | bytes 262176 | tf_op jit(solution)/shard_map/ppermute | solution.py:25
  437.1 5.5 collective-permute-start.21
  442.9 13.4 %collective-permute-start.22 = (bf16[128,1024]{0,1:T(8,128)(2,1)}, bf16[128,1024]{0,1:T(8,128)(2,1)}, u32[]{:S(2)}, u32[]{:S(2)}) collective-permute-start(bf16[128,1024]{0,1:T(8,128)(2,1)} %bitcast.15), channel_id=1, source_target_pairs={{0,16},{8,24},{16,32},{24,40},{32,48},{40,56},{48,64},{56,72},{64,... | collective-permute-start | bytes 786440 | tf_op jit(solution)/shard_map/ppermute | solution.py:25
  456.4 8.9 %collective-permute-start.23 = (bf16[128,1024]{0,1:T(8,128)(2,1)}, bf16[128,1024]{0,1:T(8,128)(2,1)}, u32[]{:S(2)}, u32[]{:S(2)}) collective-permute-start(bf16[128,1024]{0,1:T(8,128)(2,1)} %bitcast.15), channel_id=1, source_target_pairs={{0,8},{8,16},{16,24},{24,32},{32,40},{40,48},{48,56},{56,64},{64,7... | collective-permute-start | bytes 786440 | tf_op jit(solution)/shard_map/ppermute | solution.py:25
  493.2 3.7 fusion.56
  507.8 6.2 fusion.31
  513.9 18.2 %fusion = f32[24,1024]{1,0:T(8,128)S(1)} fusion(f32[168,1024]{1,0:T(8,128)} %fusion.31), kind=kCustom, calls=%all-reduce-scatter | all-reduce-scatter fusion | flops 196609 | bytes 787456
  555.8 5.8 collective-permute-done.28
  561.6 4.1 collective-permute-done.27
  565.7 9.3 %collective-permute-done.25 = bf16[128,1024]{1,0:T(8,128)(2,1)} collective-permute-done((bf16[128,1024]{1,0:T(8,128)(2,1)}, bf16[128,1024]{1,0:T(8,128)(2,1)}, u32[]{:S(2)}, u32[]{:S(2)}) %collective-permute-start.25) | collective-permute-done | bytes 262176 | tf_op jit(solution)/shard_map/ppermute | solution.py:25
  577.6 103.5 %psum.7 = f32[]{:T(128)} all-reduce(f32[]{:T(128)} %multiply_reduce_fusion), channel_id=1, replica_groups=mesh['ctx'=32,'dp'=8] {'ctx','dp'}, use_global_device_ids=true, to_apply=%region_5.6 | all-reduce | flops 1 | bytes 8 | tf_op jit(solution)/shard_map/psum | solution.py:161
  682.5 13.5 %all-gather = bf16[8,21,1024]{2,1,0:T(8,128)(2,1)S(1)} all-gather(bf16[1,21,1024]{2,1,0:T(8,128)(2,1)S(1)} %get-tuple-element.28), channel_id=1, replica_groups=mesh['ctx'=32,'dp'=8] {'dp'}, dimensions={0}, use_global_device_ids=true | all-gather | bytes 387072 | tf_op jit(solution)/shard_map/all_gather | solution.py:168
  (212 shorter events, 147.5 us)
Async XLA Ops:
  1.3 34.0 %collective-permute-start.8 = (bf16[128]{0:T(256)(128)(2,1)S(1)}, bf16[128]{0:T(256)(128)(2,1)S(1)}, u32[]{:S(2)}, u32[]{:S(2)}) collective-permute-start(bf16[128]{0:T(256)(128)(2,1)S(1)} %convert_bitcast_fusion.1), channel_id=1, source_target_pairs={{0,64},{8,72},{16,80},{24,88},{32,96},{40,104},{48,112},{56,120},{... | collective-permute-start | bytes 776 | tf_op jit(solution)/shard_map/ppermute | solution.py:25
  7.0 34.0 %collective-permute-start.9 = (bf16[128]{0:T(256)(128)(2,1)S(1)}, bf16[128]{0:T(256)(128)(2,1)S(1)}, u32[]{:S(2)}, u32[]{:S(2)}) collective-permute-start(bf16[128]{0:T(256)(128)(2,1)S(1)} %convert_bitcast_fusion.1), channel_id=1, source_target_pairs={{0,56},{8,64},{16,72},{24,80},{32,88},{40,96},{48,104},{56,112},{6... | collective-permute-start | bytes 776 | tf_op jit(solution)/shard_map/ppermute | solution.py:25
  14.5 90.9 %collective-permute-start = (bf16[128,1024]{0,1:T(8,128)(2,1)}, bf16[128,1024]{0,1:T(8,128)(2,1)S(1)}, u32[]{:S(2)}, u32[]{:S(2)}) collective-permute-start(bf16[128,1024]{0,1:T(8,128)(2,1)} %bitcast), channel_id=1, source_target_pairs={{0,64},{8,72},{16,80},{24,88},{32,96},{40,104},{48,112},{56,120},{... | collective-permute-start | bytes 786440 | tf_op jit(solution)/shard_map/ppermute | solution.py:25
  19.9 88.3 %collective-permute-start.1 = (bf16[128,1024]{0,1:T(8,128)(2,1)}, bf16[128,1024]{0,1:T(8,128)(2,1)S(1)}, u32[]{:S(2)}, u32[]{:S(2)}) collective-permute-start(bf16[128,1024]{0,1:T(8,128)(2,1)} %bitcast), channel_id=1, source_target_pairs={{0,56},{8,64},{16,72},{24,80},{32,88},{40,96},{48,104},{56,112},{6... | collective-permute-start | bytes 786440 | tf_op jit(solution)/shard_map/ppermute | solution.py:25
  23.3 87.8 %collective-permute-start.2 = (bf16[128,1024]{0,1:T(8,128)(2,1)}, bf16[128,1024]{0,1:T(8,128)(2,1)S(1)}, u32[]{:S(2)}, u32[]{:S(2)}) collective-permute-start(bf16[128,1024]{0,1:T(8,128)(2,1)} %bitcast), channel_id=1, source_target_pairs={{0,48},{8,56},{16,64},{24,72},{32,80},{40,88},{48,96},{56,104},{64... | collective-permute-start | bytes 786440 | tf_op jit(solution)/shard_map/ppermute | solution.py:25
  27.7 185.8 %all-to-all-start.1 = ((bf16[128,32,168]{0,2,1:T(8,128)(2,1)}), bf16[128,32,168]{0,2,1:T(8,128)(2,1)}, u32[]{:S(2)}, u32[]{:S(2)}) async-start(bf16[128,32,168]{0,2,1:T(8,128)(2,1)} %bitcast.61), calls=%async_computation.1 | async-start | bytes 2752512 | tf_op jit(solution)/shard_map/all_to_all | solution.py:151
  35.3 30.3 %collective-permute-start.10 = (bf16[128]{0:T(256)(128)(2,1)S(1)}, bf16[128]{0:T(256)(128)(2,1)S(1)}, u32[]{:S(2)}, u32[]{:S(2)}) collective-permute-start(bf16[128]{0:T(256)(128)(2,1)S(1)} %convert_bitcast_fusion.1), channel_id=1, source_target_pairs={{0,48},{8,56},{16,64},{24,72},{32,80},{40,88},{48,96},{56,104},{64... | collective-permute-start | bytes 776 | tf_op jit(solution)/shard_map/ppermute | solution.py:25
  41.0 34.7 %collective-permute-start.11 = (bf16[128]{0:T(256)(128)(2,1)S(1)}, bf16[128]{0:T(256)(128)(2,1)S(1)}, u32[]{:S(2)}, u32[]{:S(2)}) collective-permute-start(bf16[128]{0:T(256)(128)(2,1)S(1)} %convert_bitcast_fusion.1), channel_id=1, source_target_pairs={{0,40},{8,48},{16,56},{24,64},{32,72},{40,80},{48,88},{56,96},{64,... | collective-permute-start | bytes 776 | tf_op jit(solution)/shard_map/ppermute | solution.py:25
  65.6 24.2 %collective-permute-start.12 = (bf16[128]{0:T(256)(128)(2,1)S(1)}, bf16[128]{0:T(256)(128)(2,1)S(1)}, u32[]{:S(2)}, u32[]{:S(2)}) collective-permute-start(bf16[128]{0:T(256)(128)(2,1)S(1)} %convert_bitcast_fusion.1), channel_id=1, source_target_pairs={{0,32},{8,40},{16,48},{24,56},{32,64},{40,72},{48,80},{56,88},{64,... | collective-permute-start | bytes 776 | tf_op jit(solution)/shard_map/ppermute | solution.py:25
  94.7 23.4 %collective-permute-start.3 = (bf16[128,1024]{0,1:T(8,128)(2,1)}, bf16[128,1024]{0,1:T(8,128)(2,1)S(1)}, u32[]{:S(2)}, u32[]{:S(2)}) collective-permute-start(bf16[128,1024]{0,1:T(8,128)(2,1)} %bitcast), channel_id=1, source_target_pairs={{0,40},{8,48},{16,56},{24,64},{32,72},{40,80},{48,88},{56,96},{64,... | collective-permute-start | bytes 786440 | tf_op jit(solution)/shard_map/ppermute | solution.py:25
  147.4 43.6 %collective-permute-start.39 = (bf16[128,1024]{1,0:T(8,128)(2,1)}, bf16[128,1024]{1,0:T(8,128)(2,1)}, u32[]{:S(2)}, u32[]{:S(2)}) collective-permute-start(bf16[128,1024]{1,0:T(8,128)(2,1)} %copy.147), channel_id=1, source_target_pairs={{64,0},{72,8},{80,16},{88,24},{96,32},{104,40},{112,48},{120,56},{... | collective-permute-start | bytes 786440 | tf_op jit(solution)/shard_map/ppermute | solution.py:25
  150.5 41.8 %collective-permute-start.38 = (bf16[128,1024]{1,0:T(8,128)(2,1)}, bf16[128,1024]{1,0:T(8,128)(2,1)}, u32[]{:S(2)}, u32[]{:S(2)}) collective-permute-start(bf16[128,1024]{1,0:T(8,128)(2,1)} %copy.146), channel_id=1, source_target_pairs={{56,0},{64,8},{72,16},{80,24},{88,32},{96,40},{104,48},{112,56},{1... | collective-permute-start | bytes 786440 | tf_op jit(solution)/shard_map/ppermute | solution.py:25
  153.6 40.0 %collective-permute-start.37 = (bf16[128,1024]{1,0:T(8,128)(2,1)}, bf16[128,1024]{1,0:T(8,128)(2,1)}, u32[]{:S(2)}, u32[]{:S(2)}) collective-permute-start(bf16[128,1024]{1,0:T(8,128)(2,1)} %copy.145), channel_id=1, source_target_pairs={{48,0},{56,8},{64,16},{72,24},{80,32},{88,40},{96,48},{104,56},{11... | collective-permute-start | bytes 786440 | tf_op jit(solution)/shard_map/ppermute | solution.py:25
  156.7 39.5 %collective-permute-start.36 = (bf16[128,1024]{1,0:T(8,128)(2,1)}, bf16[128,1024]{1,0:T(8,128)(2,1)}, u32[]{:S(2)}, u32[]{:S(2)}) collective-permute-start(bf16[128,1024]{1,0:T(8,128)(2,1)} %copy.144), channel_id=1, source_target_pairs={{40,0},{48,8},{56,16},{64,24},{72,32},{80,40},{88,48},{96,56},{104... | collective-permute-start | bytes 786440 | tf_op jit(solution)/shard_map/ppermute | solution.py:25
  158.8 37.4 %collective-permute-start.35 = (bf16[128,1024]{1,0:T(8,128)(2,1)}, bf16[128,1024]{1,0:T(8,128)(2,1)}, u32[]{:S(2)}, u32[]{:S(2)}) collective-permute-start(bf16[128,1024]{1,0:T(8,128)(2,1)} %copy.143), channel_id=1, source_target_pairs={{32,0},{40,8},{48,16},{56,24},{64,32},{72,40},{80,48},{88,56},{96,... | collective-permute-start | bytes 786440 | tf_op jit(solution)/shard_map/ppermute | solution.py:25
  218.0 289.8 %all-to-all-start = ((bf16[32,128,1024]{2,1,0:T(8,128)(2,1)}), bf16[32,128,1024]{2,1,0:T(8,128)(2,1)}, u32[]{:S(2)}, u32[]{:S(2)}) async-start(bf16[32,128,1024]{2,1,0:T(8,128)(2,1)} %stack.2), calls=%async_computation | async-start | bytes 16777216 | tf_op jit(solution)/shard_map/all_to_all | solution.py:155
  249.1 188.0 %collective-permute-start.16 = (bf16[128,1024]{0,1:T(8,128)(2,1)}, bf16[128,1024]{0,1:T(8,128)(2,1)S(1)}, u32[]{:S(2)}, u32[]{:S(2)}) collective-permute-start(bf16[128,1024]{0,1:T(8,128)(2,1)} %bitcast.15), channel_id=1, source_target_pairs={{0,64},{8,72},{16,80},{24,88},{32,96},{40,104},{48,112},{56,120},{... | collective-permute-start | bytes 786440 | tf_op jit(solution)/shard_map/ppermute | solution.py:25
  253.1 189.8 %collective-permute-start.17 = (bf16[128,1024]{0,1:T(8,128)(2,1)}, bf16[128,1024]{0,1:T(8,128)(2,1)S(1)}, u32[]{:S(2)}, u32[]{:S(2)}) collective-permute-start(bf16[128,1024]{0,1:T(8,128)(2,1)} %bitcast.15), channel_id=1, source_target_pairs={{0,56},{8,64},{16,72},{24,80},{32,88},{40,96},{48,104},{56,112},{6... | collective-permute-start | bytes 786440 | tf_op jit(solution)/shard_map/ppermute | solution.py:25
  258.3 198.1 %collective-permute-start.18 = (bf16[128,1024]{0,1:T(8,128)(2,1)}, bf16[128,1024]{0,1:T(8,128)(2,1)S(1)}, u32[]{:S(2)}, u32[]{:S(2)}) collective-permute-start(bf16[128,1024]{0,1:T(8,128)(2,1)} %bitcast.15), channel_id=1, source_target_pairs={{0,48},{8,56},{16,64},{24,72},{32,80},{40,88},{48,96},{56,104},{64... | collective-permute-start | bytes 786440 | tf_op jit(solution)/shard_map/ppermute | solution.py:25
  262.9 209.6 %collective-permute-start.19 = (bf16[128,1024]{0,1:T(8,128)(2,1)}, bf16[128,1024]{0,1:T(8,128)(2,1)}, u32[]{:S(2)}, u32[]{:S(2)}) collective-permute-start(bf16[128,1024]{0,1:T(8,128)(2,1)} %bitcast.15), channel_id=1, source_target_pairs={{0,40},{8,48},{16,56},{24,64},{32,72},{40,80},{48,88},{56,96},{64,... | collective-permute-start | bytes 786440 | tf_op jit(solution)/shard_map/ppermute | solution.py:25
  266.1 208.2 %collective-permute-start.20 = (bf16[128,1024]{0,1:T(8,128)(2,1)}, bf16[128,1024]{0,1:T(8,128)(2,1)}, u32[]{:S(2)}, u32[]{:S(2)}) collective-permute-start(bf16[128,1024]{0,1:T(8,128)(2,1)} %bitcast.15), channel_id=1, source_target_pairs={{0,32},{8,40},{16,48},{24,56},{32,64},{40,72},{48,80},{56,88},{64,... | collective-permute-start | bytes 786440 | tf_op jit(solution)/shard_map/ppermute | solution.py:25
  437.1 39.0 %collective-permute-start.21 = (bf16[128,1024]{0,1:T(8,128)(2,1)}, bf16[128,1024]{0,1:T(8,128)(2,1)}, u32[]{:S(2)}, u32[]{:S(2)}) collective-permute-start(bf16[128,1024]{0,1:T(8,128)(2,1)} %bitcast.15), channel_id=1, source_target_pairs={{0,24},{8,32},{16,40},{24,48},{32,56},{40,64},{48,72},{56,80},{64,... | collective-permute-start | bytes 786440 | tf_op jit(solution)/shard_map/ppermute | solution.py:25
  442.9 35.0 %collective-permute-start.22 = (bf16[128,1024]{0,1:T(8,128)(2,1)}, bf16[128,1024]{0,1:T(8,128)(2,1)}, u32[]{:S(2)}, u32[]{:S(2)}) collective-permute-start(bf16[128,1024]{0,1:T(8,128)(2,1)} %bitcast.15), channel_id=1, source_target_pairs={{0,16},{8,24},{16,32},{24,40},{32,48},{40,56},{48,64},{56,72},{64,... | collective-permute-start | bytes 786440 | tf_op jit(solution)/shard_map/ppermute | solution.py:25
  456.4 23.3 %collective-permute-start.23 = (bf16[128,1024]{0,1:T(8,128)(2,1)}, bf16[128,1024]{0,1:T(8,128)(2,1)}, u32[]{:S(2)}, u32[]{:S(2)}) collective-permute-start(bf16[128,1024]{0,1:T(8,128)(2,1)} %bitcast.15), channel_id=1, source_target_pairs={{0,8},{8,16},{16,24},{24,32},{32,40},{40,48},{48,56},{56,64},{64,7... | collective-permute-start | bytes 786440 | tf_op jit(solution)/shard_map/ppermute | solution.py:25
  500.2 42.8 %collective-permute-start.31 = (bf16[128,1024]{1,0:T(8,128)(2,1)}, bf16[128,1024]{1,0:T(8,128)(2,1)}, u32[]{:S(2)}, u32[]{:S(2)}) collective-permute-start(bf16[128,1024]{1,0:T(8,128)(2,1)} %copy.137), channel_id=1, source_target_pairs={{64,0},{72,8},{80,16},{88,24},{96,32},{104,40},{112,48},{120,56},{... | collective-permute-start | bytes 786440 | tf_op jit(solution)/shard_map/ppermute | solution.py:25
  503.2 41.0 %collective-permute-start.30 = (bf16[128,1024]{1,0:T(8,128)(2,1)}, bf16[128,1024]{1,0:T(8,128)(2,1)}, u32[]{:S(2)}, u32[]{:S(2)}) collective-permute-start(bf16[128,1024]{1,0:T(8,128)(2,1)} %copy.136), channel_id=1, source_target_pairs={{56,0},{64,8},{72,16},{80,24},{88,32},{96,40},{104,48},{112,56},{1... | collective-permute-start | bytes 786440 | tf_op jit(solution)/shard_map/ppermute | solution.py:25
  506.3 39.4 %collective-permute-start.29 = (bf16[128,1024]{1,0:T(8,128)(2,1)}, bf16[128,1024]{1,0:T(8,128)(2,1)}, u32[]{:S(2)}, u32[]{:S(2)}) collective-permute-start(bf16[128,1024]{1,0:T(8,128)(2,1)} %copy.135), channel_id=1, source_target_pairs={{48,0},{56,8},{64,16},{72,24},{80,32},{88,40},{96,48},{104,56},{11... | collective-permute-start | bytes 786440 | tf_op jit(solution)/shard_map/ppermute | solution.py:25
  538.2 23.4 %collective-permute-start.28 = (bf16[128,1024]{1,0:T(8,128)(2,1)}, bf16[128,1024]{1,0:T(8,128)(2,1)}, u32[]{:S(2)}, u32[]{:S(2)}) collective-permute-start(bf16[128,1024]{1,0:T(8,128)(2,1)} %copy.134), channel_id=1, source_target_pairs={{40,0},{48,8},{56,16},{64,24},{72,32},{80,40},{88,48},{96,56},{104... | collective-permute-start | bytes 786440 | tf_op jit(solution)/shard_map/ppermute | solution.py:25
  542.9 22.7 %collective-permute-start.27 = (bf16[128,1024]{1,0:T(8,128)(2,1)}, bf16[128,1024]{1,0:T(8,128)(2,1)}, u32[]{:S(2)}, u32[]{:S(2)}) collective-permute-start(bf16[128,1024]{1,0:T(8,128)(2,1)} %copy.133), channel_id=1, source_target_pairs={{32,0},{40,8},{48,16},{56,24},{64,32},{72,40},{80,48},{88,56},{96,... | collective-permute-start | bytes 786440 | tf_op jit(solution)/shard_map/ppermute | solution.py:25
  544.2 21.4 %collective-permute-start.26 = (bf16[128,1024]{1,0:T(8,128)(2,1)}, bf16[128,1024]{1,0:T(8,128)(2,1)}, u32[]{:S(2)}, u32[]{:S(2)}) collective-permute-start(bf16[128,1024]{1,0:T(8,128)(2,1)} %copy.132), channel_id=1, source_target_pairs={{24,0},{32,8},{40,16},{48,24},{56,32},{64,40},{72,48},{80,56},{88,... | collective-permute-start | bytes 786440 | tf_op jit(solution)/shard_map/ppermute | solution.py:25
  545.8 29.2 %collective-permute-start.25 = (bf16[128,1024]{1,0:T(8,128)(2,1)}, bf16[128,1024]{1,0:T(8,128)(2,1)}, u32[]{:S(2)}, u32[]{:S(2)}) collective-permute-start(bf16[128,1024]{1,0:T(8,128)(2,1)} %copy.131), channel_id=1, source_target_pairs={{16,0},{24,8},{32,16},{40,24},{48,32},{56,40},{64,48},{72,56},{80,... | collective-permute-start | bytes 786440 | tf_op jit(solution)/shard_map/ppermute | solution.py:25
  547.1 27.9 %collective-permute-start.24 = (bf16[128,1024]{1,0:T(8,128)(2,1)}, bf16[128,1024]{1,0:T(8,128)(2,1)}, u32[]{:S(2)}, u32[]{:S(2)}) collective-permute-start(bf16[128,1024]{1,0:T(8,128)(2,1)} %copy.129), channel_id=1, source_target_pairs={{8,0},{16,8},{24,16},{32,24},{40,32},{48,40},{56,48},{64,56},{72,6... | collective-permute-start | bytes 786440 | tf_op jit(solution)/shard_map/ppermute | solution.py:25
  (40 other events, 1049.9 us)
